TPU v7x, 512 devices: a whole 4x8x8 slice. The times are simulated.
512 devices in a mesh: dp: 16 (over z, core), expert: 32 (over x, y).
Axes of the slice: x: 4, y: 8, z: 8, core: 2. Of those that a mesh axis runs over, the one named last changes fastest.
Arguments:
- residual_in: bfloat16 [16384, 2048], P(('dp', 'expert')), may hold values from -6 to 6
- attention_out: bfloat16 [16384, 2048], P(('dp', 'expert')), may hold values from -6 to 6
- out_weight: bfloat16 [2048, 2048], P(None, 'dp'), may hold values from -0.125 to 0.125
- post_gain: float32 [2048], replicated, may hold values from 0.1 to 1.9
- router_weight: bfloat16 [2048, 32], replicated, may hold values from -0.125 to 0.125
- expert_ids: int32 [16384, 6], P(('dp', 'expert')), may hold values from 0 to 31, all different within a row; in each aligned block of 32 rows (0 to 31, 32 to 63, ...) at most 12 rows name the same one
- expert_slot: int32 [32], replicated, may hold values from 0 to 31, each once
- expert_gate_up: bfloat16 [32, 2048, 1408], P('expert', 'dp'), may hold values from -0.125 to 0.125
- expert_down: bfloat16 [32, 704, 2048], P('expert', None, 'dp'), may hold values from -0.21875 to 0.21875
- shared_gate_up: bfloat16 [2048, 2, 2816], P(None, None, 'dp'), may hold values from -0.125 to 0.125
- shared_down: bfloat16 [2816, 2048], P(None, 'dp'), may hold values from -0.109375 to 0.109375
- final_gain: float32 [2048], replicated, may hold values from 0.1 to 1.9
Outputs:
- mixed: bfloat16 [16384, 2048], P(('dp', 'expert'))
Inputs may be any that keep to these rules, and one draw needn't show every extreme that they name: `expert_ids`: each row names 6 different experts. In each aligned block of 32 rows (the rows of one device) no expert is named by more than 12 rows, a bound that some block reaches. A permutation: expert e is held in slot expert_slot[e].
All inputs are finite; a program needn't handle non-finite values.
Results may differ from a plain program's by a relative error of at most 0.0069.
Values may be sent and summed in bfloat16 or wider, within the bound.
No kernel may reach another device: no remote copies, remote signals or barrier semaphores. Data moves between devices by JAX's collectives and lax.ppermute only.
A program may use at most 64 MiB of HBM per device.

v0:
```python
import jax
import jax.numpy as jnp
from jax import lax
from jax.sharding import PartitionSpec as P

EPS = 1e-06


def in_order(blocks, dim):
    shape = list(blocks.shape[1:])
    shape[dim] *= blocks.shape[0]
    return jnp.moveaxis(blocks, 0, dim).reshape(shape)


def sent_to_all(array, axis):
    copies = jnp.broadcast_to(array, (lax.axis_size(axis), *array.shape))
    return lax.all_to_all(copies, axis, split_axis=0, concat_axis=0, tiled=True)


def collect(array, axis, dim):
    return in_order(sent_to_all(array, axis), dim)


def turned_gather(arrays, axis, dims):
    turned = [jnp.moveaxis(a, dim, 0) for a, dim in zip(arrays, dims)]
    widths = [t[0].size for t in turned]
    both = jnp.concatenate([t.reshape(-1, w) for t, w in zip(turned, widths)], axis=1)
    out = lax.all_gather(both, axis, axis=0, tiled=True)
    blocks = jnp.split(out, [sum(widths[:k]) for k in range(1, len(widths))], axis=1)
    return tuple(
        (
            jnp.moveaxis(b.reshape(-1, *t.shape[1:]), 0, dim)
            for b, t, dim in zip(blocks, turned, dims)
        )
    )


def rms_scale(values, gain):
    values = values.astype(jnp.float32)
    inverse = lax.rsqrt(jnp.mean(values * values, axis=-1, keepdims=True) + EPS)
    return values * inverse * gain


def per_device(
    residual_in,
    attention_out,
    out_weight,
    post_gain,
    router_weight,
    expert_ids,
    expert_slot,
    expert_gate_up,
    expert_down,
    shared_gate_up,
    shared_down,
    final_gain,
):
    rows = residual_in.shape[0]
    width = residual_in.shape[1]
    experts = router_weight.shape[1]
    choose = expert_ids.shape[1]
    capacity = max(2, min(rows, 2 * rows * choose // experts))
    proj_cols = jnp.dot(
        collect(attention_out, "dp", 0), out_weight, preferred_element_type=jnp.float32
    ).astype(jnp.bfloat16)
    proj = lax.all_to_all(proj_cols, "dp", split_axis=0, concat_axis=1, tiled=True)
    resid = (residual_in.astype(jnp.float32) + proj.astype(jnp.float32)).astype(jnp.bfloat16)
    normed = rms_scale(resid, post_gain).astype(jnp.bfloat16)
    logits = jnp.dot(normed, router_weight, preferred_element_type=jnp.float32)
    expert_range = jnp.arange(experts, dtype=jnp.int32)
    picked = expert_ids[:, :, None] == expert_range[None, None, :]
    chosen = jnp.sum(jnp.where(picked, logits[:, None, :], 0.0), axis=2)
    raised = jnp.exp(chosen)
    gates = raised / jnp.sum(raised, axis=1, keepdims=True)
    slots = jnp.sum(jnp.where(picked, expert_slot[None, None, :], 0), axis=2).reshape(-1)
    marked = (slots[:, None] == expert_range[None, :]).astype(jnp.int32)
    before = jnp.cumsum(marked, axis=0) - marked
    position = jnp.sum(before * marked, axis=1)
    target = slots * capacity + position
    placed = target[:, None] == jnp.arange(experts * capacity, dtype=jnp.int32)[None, :]
    select = jnp.any(placed.reshape(rows, choose, experts * capacity), axis=1).astype(jnp.bfloat16)
    outgoing = jnp.einsum("rs,rd->sd", select, normed, preferred_element_type=jnp.float32)
    outgoing = outgoing.astype(jnp.bfloat16).reshape(experts, capacity, width)
    gate_up_all, down_all = turned_gather((expert_gate_up, expert_down), "dp", (1, 2))
    gate_up_full = gate_up_all[0]
    down_full = down_all[0]
    hidden_units = gate_up_full.shape[1] // 2
    received = lax.all_to_all(outgoing, "expert", split_axis=0, concat_axis=0, tiled=True)
    sources, count, _ = received.shape
    flat = received.reshape(sources * count, width)
    both = jnp.dot(flat, gate_up_full, preferred_element_type=jnp.float32)
    active = (jax.nn.silu(both[:, :hidden_units]) * both[:, hidden_units:]).astype(jnp.bfloat16)
    result = jnp.dot(active, down_full, preferred_element_type=jnp.float32).astype(jnp.bfloat16)
    result = result.reshape(sources, count, width)
    returned = lax.all_to_all(result, "expert", split_axis=0, concat_axis=0, tiled=True)
    shared_units = shared_gate_up.shape[2]
    shared_pair = shared_gate_up.reshape(width, 2 * shared_units)
    both = jnp.dot(
        lax.all_gather(normed, "dp", axis=0, tiled=True),
        shared_pair,
        preferred_element_type=jnp.float32,
    )
    shared_hidden = (jax.nn.silu(both[:, :shared_units]) * both[:, shared_units:]).astype(
        jnp.bfloat16
    )
    out_cols = jnp.dot(
        lax.all_gather(shared_hidden, "dp", axis=1, tiled=True),
        shared_down,
        preferred_element_type=jnp.float32,
    )
    shared_out = lax.all_to_all(out_cols, "dp", split_axis=0, concat_axis=1, tiled=True)
    back_rows = jnp.take(returned.reshape(experts * capacity, width), target, axis=0)
    back_rows = back_rows.reshape(rows, choose, width).astype(jnp.float32)
    routed = jnp.sum(gates[:, :, None] * back_rows, axis=1)
    total = resid.astype(jnp.float32) + routed + shared_out
    return rms_scale(total, final_gain).astype(jnp.bfloat16)


def solution(mesh):
    in_specs = (
        P(("dp", "expert"), None),
        P(("dp", "expert"), None),
        P(None, "dp"),
        P(),
        P(),
        P(("dp", "expert"), None),
        P(),
        P("expert", "dp", None),
        P("expert", None, "dp"),
        P(None, None, "dp"),
        P(None, "dp"),
        P(),
    )
    out_specs = P(("dp", "expert"), None)
    return jax.shard_map(
        per_device, mesh=mesh, in_specs=in_specs, out_specs=out_specs, check_vma=False
    )
```

profile of v0, /device:TPU:1, one launch (start us, length us, event | category | flops | bytes accessed | tf_op | source)
XLA Modules:
  0.0 282.8 jit_solution(13538233987763280168)
XLA Ops:
  6.5 1.3 broadcast_in_dim.50
  7.8 62.8 %all_to_all.47 = bf16[16,32,2048]{2,1,0:T(8,128)(2,1)S(1)} all-to-all(bf16[16,32,2048]{2,1,0:T(8,128)(2,1)S(1)} %broadcast_in_dim.50), channel_id=1, replica_groups=mesh['dp'=16,'expert'=32] {'dp'}, dimensions={0} | all-to-all | bytes 4194304 | tf_op jit(solution)/shard_map/all_to_all | solution.py:17
  70.6 0.7 convolution_convert_fusion.1
  71.4 11.9 %all_to_all.48 = bf16[16,32,128]{2,1,0:T(8,128)(2,1)S(1)} all-to-all(bf16[16,32,128]{2,1,0:T(8,128)(2,1)S(1)} %bitcast.66), channel_id=1, replica_groups=mesh['dp'=16,'expert'=32] {'dp'}, dimensions={0} | all-to-all | bytes 262144 | tf_op jit(solution)/shard_map/all_to_all | solution.py:66
  83.2 0.2 fusion.9
  83.4 0.6 copy-done.2
  84.0 0.8 fusion.11
  84.9 0.1 copy.30
  85.0 0.9 pad_maximum_fusion
  85.9 0.3 select_reduce_fusion
  86.3 0.1 reshape.144
  86.4 0.6 reduce-window.6
  87.0 0.2 slice_reduce_fusion
  87.6 0.6 compare_and_fusion
  88.3 0.6 convolution_convert_fusion
  88.9 1.6 reshape.147
  90.6 9.7 %all-to-all-start.2 = ((bf16[32,12,2048]{2,1,0:T(8,128)(2,1)}), bf16[32,12,2048]{2,1,0:T(8,128)(2,1)S(1)}, u32[]{:S(2)}, u32[]{:S(2)}) async-start(bf16[32,12,2048]{2,1,0:T(8,128)(2,1)} %reshape.147), calls=%async_computation.2 | async-start | bytes 4194304 | tf_op jit(solution)/shard_map/all_to_all | solution.py:88
  100.3 24.4 %all-gather.6.cloned.1.call-done = bf16[512,2048]{1,0:T(8,128)(2,1)} async-done(((bf16[32,2048]{1,0:T(8,128)(2,1)}), bf16[512,2048]{1,0:T(8,128)(2,1)}) %all-gather.6.cloned.1.call-update) | async-done | bytes 2097168 | tf_op jit(solution)/shard_map/all_gather | solution.py:99
  124.7 2.5 fusion.21
  127.3 0.8 fusion.7
  128.1 22.2 %all-to-all-done.2 = bf16[32,12,2048]{2,1,0:T(8,128)(2,1)S(1)} async-done(((bf16[32,12,2048]{2,1,0:T(8,128)(2,1)}), bf16[32,12,2048]{2,1,0:T(8,128)(2,1)S(1)}, u32[]{:S(2)}, u32[]{:S(2)}) %all-to-all-start.2) | async-done | bytes 1572896 | tf_op jit(solution)/shard_map/all_to_all | solution.py:88
  150.2 1.4 reshape.148
  151.7 35.1 %all-gather.4.cloned.1.call-done = bf16[2048,2112]{1,0:T(8,128)(2,1)} async-done(((bf16[128,2112]{1,0:T(8,128)(2,1)}), bf16[2048,2112]{1,0:T(8,128)(2,1)}) %all-gather.4.cloned.1.call-update) | async-done | bytes 8650768 | tf_op jit(solution)/shard_map/all_gather | solution.py:28
  186.8 5.7 %fusion = f32[384,1408]{1,0:T(8,128)S(1)} fusion(bf16[384,2048]{1,0:T(8,128)(2,1)} %reshape.148, bf16[2048,2112]{1,0:T(8,128)(2,1)} %all-gather.4.cloned.1.call-done), kind=kOutput, calls=%fused_computation.1 | convolution fusion | flops 2214592512 | bytes 9502720 | tf_op jit(solution)/shard_map/dot_general | solution.py:91
  192.5 3.3 %fusion.3 = bf16[384,2048]{1,0:T(8,128)(2,1)S(1)} fusion(bf16[2048,2112]{1,0:T(8,128)(2,1)} %all-gather.4.cloned.1.call-done, f32[384,1408]{1,0:T(8,128)S(1)} %fusion), kind=kOutput, calls=%fused_computation.5 | convolution fusion | flops 1109704704 | bytes 7077888 | tf_op jit(solution)/shard_map/dot_general | solution.py:93
  195.8 1.5 reshape.151
  197.4 9.3 %all-to-all-start.3 = ((bf16[32,12,2048]{2,1,0:T(8,128)(2,1)}), bf16[32,12,2048]{2,1,0:T(8,128)(2,1)S(1)}, u32[]{:S(2)}, u32[]{:S(2)}) async-start(bf16[32,12,2048]{2,1,0:T(8,128)(2,1)} %reshape.151), calls=%async_computation.3 | async-start | bytes 4194304 | tf_op jit(solution)/shard_map/all_to_all | solution.py:95
  206.6 0.6 broadcast_multiply_fusion
  207.2 0.8 copy.31
  208.0 0.7 mul.96
  208.6 1.3 copy.29
  210.0 0.7 compare_select_fusion.1
  210.7 0.6 pad_clamp_fusion
  211.3 1.1 fusion.20
  212.4 0.9 select_reduce_fusion.1
  213.3 17.8 %all-gather.8.cloned.1.call-done = bf16[512,2816]{0,1:T(8,128)(2,1)} async-done(((bf16[512,176]{0,1:T(8,128)(2,1)}), bf16[512,2816]{0,1:T(8,128)(2,1)}) %all-gather.8.cloned.1.call-update) | async-done | bytes 2883600 | tf_op jit(solution)/shard_map/all_gather | solution.py:107
  231.1 3.6 %fusion.22 = f32[512,128]{1,0:T(8,128)} fusion(bf16[512,2816]{0,1:T(8,128)(2,1)} %all-gather.8.cloned.1.call-done, bf16[2816,128]{1,0:T(8,128)(2,1)} %param.22), kind=kOutput, calls=%fused_computation.55 | convolution fusion | flops 369098752 | bytes 3866624 | tf_op jit(solution)/shard_map/dot_general | solution.py:106
  234.8 20.8 %all-to-all-done.3 = bf16[32,12,2048]{2,1,0:T(8,128)(2,1)S(1)} async-done(((bf16[32,12,2048]{2,1,0:T(8,128)(2,1)}), bf16[32,12,2048]{2,1,0:T(8,128)(2,1)S(1)}, u32[]{:S(2)}, u32[]{:S(2)}) %all-to-all-start.3) | async-done | bytes 1572896 | tf_op jit(solution)/shard_map/all_to_all | solution.py:95
  255.5 6.1 %all-to-all-start.4 = ((f32[16,32,128]{2,1,0:T(8,128)}), f32[16,32,128]{2,1,0:T(8,128)}, u32[]{:S(2)}, u32[]{:S(2)}) async-start(f32[16,32,128]{2,1,0:T(8,128)} %bitcast.65), calls=%async_computation.4 | async-start | bytes 524288 | tf_op jit(solution)/shard_map/all_to_all | solution.py:111
  261.7 0.6 exponential_divide_fusion
  262.3 0.8 copy.24
  263.0 2.5 reshape.152
  265.6 2.2 gather_fusion
  267.7 1.4 gather.7
  269.1 1.7 multiply_reduce_fusion
  270.8 2.7 all-to-all-done.4
  273.5 1.1 multiply_reduce_fusion.1
  274.6 1.7 multiply_convert_fusion
  (48 shorter events, 0.8 us)
Async XLA Ops:
  6.5 118.2 %copy-start = (bf16[2048,2,176]{0,2,1:T(8,128)(2,1)S(1)}, bf16[2048,2,176]{0,2,1:T(8,128)(2,1)}, u32[]{:S(2)}) copy-start(bf16[2048,2,176]{0,2,1:T(8,128)(2,1)} %param.21) | copy-start | bytes 4325380
  6.5 118.2 %all-gather.6.cloned.1.call-start = ((), (), s32[]{:S(2)}) async-start(), calls=%async_computation.6 | async-start | bytes 2228224 | tf_op jit(solution)/shard_map/all_gather | solution.py:99
  7.8 62.8 %copy-start.5 = (bf16[2048,128]{1,0:T(8,128)(2,1)S(1)}, bf16[2048,128]{1,0:T(8,128)(2,1)}, u32[]{:S(2)}) copy-start(bf16[2048,128]{1,0:T(8,128)(2,1)} %param.14) | copy-start | bytes 1572868
  70.6 12.6 %copy-start.8 = (bf16[32,2048]{1,0:T(8,128)(2,1)S(1)}, bf16[32,2048]{1,0:T(8,128)(2,1)}, u32[]{:S(2)}) copy-start(bf16[32,2048]{1,0:T(8,128)(2,1)} %param.12) | copy-start | bytes 393220
  70.6 13.4 %copy-start.13 = (f32[2048]{0:T(1024)S(1)}, f32[2048]{0:T(1024)}, u32[]{:S(2)}) copy-start(f32[2048]{0:T(1024)} %param.15) | copy-start | bytes 24580
  70.6 14.3 %copy-start.7 = (bf16[1,704,128]{2,1,0:T(8,128)(2,1)S(1)}, bf16[1,704,128]{2,1,0:T(8,128)(2,1)}, u32[]{:S(2)}) copy-start(bf16[1,704,128]{2,1,0:T(8,128)(2,1)} %param.20) | copy-start | bytes 540676
  70.6 14.4 %copy-start.6 = (bf16[1,128,1408]{2,1,0:T(8,128)(2,1)S(1)}, bf16[1,128,1408]{2,1,0:T(8,128)(2,1)}, u32[]{:S(2)}) copy-start(bf16[1,128,1408]{2,1,0:T(8,128)(2,1)} %param.19) | copy-start | bytes 1081348
  71.3 14.6 %copy-start.10 = (s32[32,6]{0,1:T(8,128)S(1)}, s32[32,6]{0,1:T(8,128)}, u32[]{:S(2)}) copy-start(s32[32,6]{0,1:T(8,128)} %param.17) | copy-start | bytes 2308
  71.3 14.6 %copy-start.14 = (s32[32]{0:T(128)S(1)}, s32[32]{0:T(128)}, u32[]{:S(2)}) copy-start(s32[32]{0:T(128)} %param.18) | copy-start | bytes 388
  83.4 0.6 copy-start.2
  84.8 3.5 %copy-start.4 = (bf16[32,2048]{1,0:T(8,128)(2,1)S(1)}, bf16[32,2048]{1,0:T(8,128)(2,1)}, u32[]{:S(2)}) copy-start(bf16[32,2048]{1,0:T(8,128)(2,1)} %fusion.11) | copy-start | bytes 393220
  84.8 101.9 %all-gather.4.cloned.1.call-start = ((), (), s32[]{:S(2)}) async-start(), calls=%async_computation.5 | async-start | bytes 9469952 | tf_op jit(solution)/shard_map/all_gather | solution.py:28
  87.4 0.8 copy-start.11
  90.6 59.7 %all-to-all-start.2 = ((bf16[32,12,2048]{2,1,0:T(8,128)(2,1)}), bf16[32,12,2048]{2,1,0:T(8,128)(2,1)S(1)}, u32[]{:S(2)}, u32[]{:S(2)}) async-start(bf16[32,12,2048]{2,1,0:T(8,128)(2,1)} %reshape.147), calls=%async_computation.2 | async-start | bytes 4194304 | tf_op jit(solution)/shard_map/all_to_all | solution.py:88
  100.2 130.9 %all-gather.8.cloned.1.call-start = ((), (), s32[]{:S(2)}) async-start(), calls=%async_computation.7 | async-start | bytes 3063808 | tf_op jit(solution)/shard_map/all_gather | solution.py:107
  197.4 58.2 %all-to-all-start.3 = ((bf16[32,12,2048]{2,1,0:T(8,128)(2,1)}), bf16[32,12,2048]{2,1,0:T(8,128)(2,1)S(1)}, u32[]{:S(2)}, u32[]{:S(2)}) async-start(bf16[32,12,2048]{2,1,0:T(8,128)(2,1)} %reshape.151), calls=%async_computation.3 | async-start | bytes 4194304 | tf_op jit(solution)/shard_map/all_to_all | solution.py:95
  255.5 6.7 %copy-start.1 = (bf16[32,12,2048]{2,1,0:T(8,128)(2,1)}, bf16[32,12,2048]{2,1,0:T(8,128)(2,1)S(1)}, u32[]{:S(2)}) copy-start(bf16[32,12,2048]{2,1,0:T(8,128)(2,1)S(1)} %all-to-all-done.3) | copy-start | bytes 4718596
  255.5 18.0 %all-to-all-start.4 = ((f32[16,32,128]{2,1,0:T(8,128)}), f32[16,32,128]{2,1,0:T(8,128)}, u32[]{:S(2)}, u32[]{:S(2)}) async-start(f32[16,32,128]{2,1,0:T(8,128)} %bitcast.65), calls=%async_computation.4 | async-start | bytes 524288 | tf_op jit(solution)/shard_map/all_to_all | solution.py:111
  265.5 3.6 %copy-start.9 = (pred[32,6]{1,0:T(8,128)(4,1)S(1)}, pred[32,6]{1,0:T(8,128)(4,1)}, u32[]{:S(2)}) copy-start(pred[32,6]{1,0:T(8,128)(4,1)} %copy.29) | copy-start | bytes 580
  267.7 5.8 %copy-start.3 = (bf16[32,2048]{1,0:T(8,128)(2,1)S(1)}, bf16[32,2048]{1,0:T(8,128)(2,1)}, u32[]{:S(2)}) copy-start(bf16[32,2048]{1,0:T(8,128)(2,1)} %copy-done.2) | copy-start | bytes 393220
  267.7 6.9 %copy-start.12 = (f32[2048]{0:T(1024)S(1)}, f32[2048]{0:T(1024)}, u32[]{:S(2)}) copy-start(f32[2048]{0:T(1024)} %param.23) | copy-start | bytes 24580
Sparse Core Ops, SparseCore 0:
  84.9 39.7 all-gather.5
  126.8 59.8 all-gather.3
  188.9 42.1 all-gather.7
where the time goes:
time: 284 us; the launch traced here: 283 us
  waiting for transfers between devices  123 us (43%)
  blocking collectives  74.6 us (26%)
  starting transfers between devices  25.1 us (9%)
  matrix products  17.7 us (6%)
  local copies, waits for them, and re-layouts  16.8 us (6%)
  between operations  13.4 us (5%)
  other arithmetic  12.2 us (4%)
    all_to_all x1, blocking collectives, sent_to_all(): return lax.all_to_all(copies, axis, split_axis=0, concat_axis=0, tiled=True)  62.8 us
    all_gather x1, waiting for transfers between devices, turned_gather(): out = lax.all_gather(both, axis, axis=0, tiled=True)  35.1 us
    all_gather x1, waiting for transfers between devices, per_device(): lax.all_gather(normed, 'dp', axis=0, tiled=True)  24.4 us
    all_to_all x1, waiting for transfers between devices, per_device(): lax.all_to_all(outgoing, 'expert', split_axis=0, concat_axis=0, tiled=True)  22.2 us
    all_to_all x1, waiting for transfers between devices, per_device(): lax.all_to_all(result, 'expert', split_axis=0, concat_axis=0, tiled=True)  20.8 us
    all_gather x1, waiting for transfers between devices, per_device(): lax.all_gather(shared_hidden, 'dp', axis=1, tiled=True)  17.8 us
    all_to_all x1, blocking collectives, per_device(): lax.all_to_all(proj_cols, 'dp', split_axis=0, concat_axis=1, tiled=True)  11.9 us
    all_to_all x1, starting transfers between devices, per_device(): lax.all_to_all(outgoing, 'expert', split_axis=0, concat_axis=0, tiled=True)  9.67 us
  transfers between devices with their start and end apart: 6, of which 6 were waited for; matrix products, arithmetic and copies ran while one was open for 14% of the time, Pallas kernels for 0%

commit v1 on v0

--- a/solution.py
+++ b/solution.py
@@ -104,7 +104,9 @@
         jnp.bfloat16
     )
     out_cols = jnp.dot(
-        lax.all_gather(shared_hidden, "dp", axis=1, tiled=True),
+        jnp.concatenate(
+            lax.all_to_all(jnp.stack([shared_hidden] * lax.axis_size("dp")), "dp", 0, 0), axis=1
+        ),
         shared_down,
         preferred_element_type=jnp.float32,
     )

time: 284 us -> 346 us (1.22)
  waiting for transfers between devices: 123 us -> 161 us
  local copies, waits for them, and re-layouts: 16.8 us -> 35.6 us
  starting transfers between devices: 25.1 us -> 30.1 us
    all_gather x1, waiting for transfers between devices: 35.1 us -> 89 us  [turned_gather(): out = lax.all_gather(both, axis, axis=0, tiled=True)]
    all_gather x1 -> x0, waiting for transfers between devices: 17.8 us -> none  [per_device(): lax.all_gather(shared_hidden, 'dp', axis=1, tiled=True)]
    dot_general x0 -> x1, local copies, waits for them, and re-layouts: none -> 8.38 us  [per_device(): jnp.dot(jnp.concatenate(lax.all_to_all(jnp.stack([shared_hidden] * lax.ax...]
    reshape x0 -> x1, local copies, waits for them, and re-layouts: none -> 7.63 us  [per_device(): jnp.concatenate(lax.all_to_all(jnp.stack([shared_hidden] * lax.axis_size(...]
    all_to_all x0 -> x1, starting transfers between devices: none -> 4.95 us  [per_device(): lax.all_to_all(jnp.stack([shared_hidden] * lax.axis_size('dp')), 'dp', 0, 0)]
  transfers between devices with their start and end apart: 6 -> 6, of which waited for: 6 -> 5; matrix products, arithmetic and copies ran while one was open for 14% -> 17% of each run, Pallas kernels for 0% -> 0%
where the time goes in v1:
time: 346 us; the launch traced here: 345 us
  waiting for transfers between devices  161 us (47%)
  blocking collectives  74.6 us (22%)
  local copies, waits for them, and re-layouts  35.6 us (10%)
  starting transfers between devices  30.1 us (9%)
  matrix products  17.6 us (5%)
  between operations  13.7 us (4%)
  other arithmetic  12.1 us (3%)
    all_gather x1, waiting for transfers between devices, turned_gather(): out = lax.all_gather(both, axis, axis=0, tiled=True)  89 us
    all_to_all x1, blocking collectives, sent_to_all(): return lax.all_to_all(copies, axis, split_axis=0, concat_axis=0, tiled=True)  62.8 us
    all_gather x1, waiting for transfers between devices, per_device(): lax.all_gather(normed, 'dp', axis=0, tiled=True)  24.6 us
    all_to_all x1, waiting for transfers between devices, per_device(): lax.all_to_all(result, 'expert', split_axis=0, concat_axis=0, tiled=True)  22.6 us
    all_to_all x1, waiting for transfers between devices, per_device(): lax.all_to_all(outgoing, 'expert', split_axis=0, concat_axis=0, tiled=True)  22.1 us
    all_to_all x1, blocking collectives, per_device(): lax.all_to_all(proj_cols, 'dp', split_axis=0, concat_axis=1, tiled=True)  11.9 us
    all_to_all x1, starting transfers between devices, per_device(): lax.all_to_all(outgoing, 'expert', split_axis=0, concat_axis=0, tiled=True)  9.67 us
    all_to_all x1, starting transfers between devices, per_device(): lax.all_to_all(result, 'expert', split_axis=0, concat_axis=0, tiled=True)  9.55 us
  transfers between devices with their start and end apart: 6, of which 5 were waited for; matrix products, arithmetic and copies ran while one was open for 17% of the time, Pallas kernels for 0%

profile of v1, /device:TPU:1, one launch (start us, length us, event | category | flops | bytes accessed | tf_op | source)
XLA Modules:
  0.0 344.9 jit_solution(6094091933552486599)
XLA Ops:
  6.5 1.3 broadcast_in_dim.50
  7.8 62.8 %all_to_all.49 = bf16[16,32,2048]{2,1,0:T(8,128)(2,1)S(1)} all-to-all(bf16[16,32,2048]{2,1,0:T(8,128)(2,1)S(1)} %broadcast_in_dim.50), channel_id=1, replica_groups=mesh['dp'=16,'expert'=32] {'dp'}, dimensions={0} | all-to-all | bytes 4194304 | tf_op jit(solution)/shard_map/all_to_all | solution.py:17
  70.6 0.7 convolution_convert_fusion.1
  71.4 11.9 %all_to_all.50 = bf16[16,32,128]{2,1,0:T(8,128)(2,1)S(1)} all-to-all(bf16[16,32,128]{2,1,0:T(8,128)(2,1)S(1)} %bitcast.67), channel_id=1, replica_groups=mesh['dp'=16,'expert'=32] {'dp'}, dimensions={0} | all-to-all | bytes 262144 | tf_op jit(solution)/shard_map/all_to_all | solution.py:66
  83.4 0.6 copy-done.2
  84.0 0.8 fusion.13
  85.0 0.9 pad_maximum_fusion
  85.9 0.3 select_reduce_fusion
  86.4 0.6 reduce-window.6
  87.0 0.2 slice_reduce_fusion
  87.6 0.6 compare_and_fusion
  88.3 0.6 convolution_convert_fusion
  88.9 1.5 reshape.155
  90.4 9.7 %all-to-all-start.2 = ((bf16[32,12,2048]{2,1,0:T(8,128)(2,1)}), bf16[32,12,2048]{2,1,0:T(8,128)(2,1)S(1)}, u32[]{:S(2)}, u32[]{:S(2)}) async-start(bf16[32,12,2048]{2,1,0:T(8,128)(2,1)} %reshape.155), calls=%async_computation.2 | async-start | bytes 4194304 | tf_op jit(solution)/shard_map/all_to_all | solution.py:88
  100.1 24.6 %all-gather.5.cloned.1.call-done = bf16[512,2048]{1,0:T(8,128)(2,1)} async-done(((bf16[32,2048]{1,0:T(8,128)(2,1)}), bf16[512,2048]{1,0:T(8,128)(2,1)}) %all-gather.5.cloned.1.call-update) | async-done | bytes 2097168 | tf_op jit(solution)/shard_map/all_gather | solution.py:99
  124.7 2.5 fusion.23
  127.2 0.8 fusion.9
  128.0 22.1 %all-to-all-done.2 = bf16[32,12,2048]{2,1,0:T(8,128)(2,1)S(1)} async-done(((bf16[32,12,2048]{2,1,0:T(8,128)(2,1)}), bf16[32,12,2048]{2,1,0:T(8,128)(2,1)S(1)}, u32[]{:S(2)}, u32[]{:S(2)}) %all-to-all-start.2) | async-done | bytes 1572896 | tf_op jit(solution)/shard_map/all_to_all | solution.py:88
  150.1 2.9 stack.2
  153.0 5.0 %all-to-all-start.4 = ((bf16[16,512,176]{1,2,0:T(8,128)(2,1)}), bf16[16,512,176]{1,2,0:T(8,128)(2,1)}, u32[]{:S(2)}, u32[]{:S(2)}) async-start(bf16[16,512,176]{1,2,0:T(8,128)(2,1)} %stack.2), calls=%async_computation.4 | async-start | bytes 5767168 | tf_op jit(solution)/shard_map/all_to_all | solution.py:108
  157.9 1.4 reshape.156
  159.3 89.0 %all-gather.3.cloned.1.call-done = bf16[2048,2112]{1,0:T(8,128)(2,1)} async-done(((bf16[128,2112]{1,0:T(8,128)(2,1)}), bf16[2048,2112]{1,0:T(8,128)(2,1)}) %all-gather.3.cloned.1.call-update) | async-done | bytes 8650768 | tf_op jit(solution)/shard_map/all_gather | solution.py:28
  248.3 5.7 %fusion = f32[384,1408]{1,0:T(8,128)S(1)} fusion(bf16[384,2048]{1,0:T(8,128)(2,1)} %reshape.156, bf16[2048,2112]{1,0:T(8,128)(2,1)} %all-gather.3.cloned.1.call-done), kind=kOutput, calls=%fused_computation.1 | convolution fusion | flops 2214592512 | bytes 9502720 | tf_op jit(solution)/shard_map/dot_general | solution.py:91
  254.0 3.3 fusion.3
  257.3 1.5 reshape.159
  258.9 9.5 %all-to-all-start.3 = ((bf16[32,12,2048]{2,1,0:T(8,128)(2,1)}), bf16[32,12,2048]{2,1,0:T(8,128)(2,1)S(1)}, u32[]{:S(2)}, u32[]{:S(2)}) async-start(bf16[32,12,2048]{2,1,0:T(8,128)(2,1)} %reshape.159), calls=%async_computation.3 | async-start | bytes 4194304 | tf_op jit(solution)/shard_map/all_to_all | solution.py:95
  268.4 0.6 broadcast_multiply_fusion
  269.0 0.8 copy.39
  269.8 0.7 mul.96
  270.5 1.3 copy.37
  271.8 0.7 compare_select_fusion.1
  272.5 0.6 pad_clamp_fusion
  273.1 1.1 fusion.22
  274.2 0.9 select_reduce_fusion.1
  275.1 7.6 %copy.40 = bf16[512,16,176]{2,1,0:T(8,128)(2,1)} copy(bf16[512,16,176]{0,2,1:T(8,128)(2,1)} %bitcast.13) | data formatting | bytes 5767168 | tf_op jit(solution)/shard_map/reshape | solution.py:107
  282.7 8.4 %dot_general.29 = bf16[16,32,2816]{2,1,0:T(8,128)(2,1)} reshape(bf16[512,16,176]{2,1,0:T(8,128)(2,1)} %copy.40) | data formatting | bytes 5767168 | tf_op jit(solution)/shard_map/dot_general | solution.py:106
  291.1 3.6 %fusion.5 = f32[16,32,128]{2,1,0:T(8,128)} fusion(bf16[16,32,2816]{2,1,0:T(8,128)(2,1)} %dot_general.29, bf16[2816,128]{1,0:T(8,128)(2,1)} %param.22), kind=kOutput, calls=%fused_computation.11 | convolution fusion | flops 369098752 | bytes 3866624 | tf_op jit(solution)/shard_map/dot_general | solution.py:106
  294.7 22.6 %all-to-all-done.3 = bf16[32,12,2048]{2,1,0:T(8,128)(2,1)S(1)} async-done(((bf16[32,12,2048]{2,1,0:T(8,128)(2,1)}), bf16[32,12,2048]{2,1,0:T(8,128)(2,1)S(1)}, u32[]{:S(2)}, u32[]{:S(2)}) %all-to-all-start.3) | async-done | bytes 1572896 | tf_op jit(solution)/shard_map/all_to_all | solution.py:95
  317.3 5.9 %all-to-all-start.5 = ((f32[16,32,128]{2,1,0:T(8,128)}), f32[16,32,128]{2,1,0:T(8,128)}, u32[]{:S(2)}, u32[]{:S(2)}) async-start(f32[16,32,128]{2,1,0:T(8,128)} %fusion.5), calls=%async_computation.5 | async-start | bytes 524288 | tf_op jit(solution)/shard_map/all_to_all | solution.py:113
  323.3 0.6 exponential_divide_fusion
  323.9 0.8 copy.32
  324.7 2.5 reshape.160
  327.2 2.2 gather_fusion
  329.3 1.4 gather.7
  330.7 1.7 multiply_reduce_fusion
  332.4 2.8 all-to-all-done.5
  335.2 1.1 multiply_reduce_fusion.1
  336.4 1.7 multiply_convert_fusion
  (50 shorter events, 1.1 us)
Async XLA Ops:
  6.5 118.1 %copy-start = (bf16[2048,2,176]{0,2,1:T(8,128)(2,1)S(1)}, bf16[2048,2,176]{0,2,1:T(8,128)(2,1)}, u32[]{:S(2)}) copy-start(bf16[2048,2,176]{0,2,1:T(8,128)(2,1)} %param.21) | copy-start | bytes 4325380
  6.5 118.1 %all-gather.5.cloned.1.call-start = ((), (), s32[]{:S(2)}) async-start(), calls=%async_computation.7 | async-start | bytes 2228224 | tf_op jit(solution)/shard_map/all_gather | solution.py:99
  7.8 62.8 %copy-start.5 = (bf16[2048,128]{1,0:T(8,128)(2,1)S(1)}, bf16[2048,128]{1,0:T(8,128)(2,1)}, u32[]{:S(2)}) copy-start(bf16[2048,128]{1,0:T(8,128)(2,1)} %param.14) | copy-start | bytes 1572868
  70.6 12.6 %copy-start.8 = (bf16[32,2048]{1,0:T(8,128)(2,1)S(1)}, bf16[32,2048]{1,0:T(8,128)(2,1)}, u32[]{:S(2)}) copy-start(bf16[32,2048]{1,0:T(8,128)(2,1)} %param.12) | copy-start | bytes 393220
  70.6 13.4 %copy-start.13 = (f32[2048]{0:T(1024)S(1)}, f32[2048]{0:T(1024)}, u32[]{:S(2)}) copy-start(f32[2048]{0:T(1024)} %param.15) | copy-start | bytes 24580
  70.6 14.3 %copy-start.7 = (bf16[1,704,128]{2,1,0:T(8,128)(2,1)S(1)}, bf16[1,704,128]{2,1,0:T(8,128)(2,1)}, u32[]{:S(2)}) copy-start(bf16[1,704,128]{2,1,0:T(8,128)(2,1)} %param.20) | copy-start | bytes 540676
  70.6 14.4 %copy-start.6 = (bf16[1,128,1408]{2,1,0:T(8,128)(2,1)S(1)}, bf16[1,128,1408]{2,1,0:T(8,128)(2,1)}, u32[]{:S(2)}) copy-start(bf16[1,128,1408]{2,1,0:T(8,128)(2,1)} %param.19) | copy-start | bytes 1081348
  71.3 14.6 %copy-start.10 = (s32[32,6]{0,1:T(8,128)S(1)}, s32[32,6]{0,1:T(8,128)}, u32[]{:S(2)}) copy-start(s32[32,6]{0,1:T(8,128)} %param.17) | copy-start | bytes 2308
  71.3 14.6 %copy-start.14 = (s32[32]{0:T(128)S(1)}, s32[32]{0:T(128)}, u32[]{:S(2)}) copy-start(s32[32]{0:T(128)} %param.18) | copy-start | bytes 388
  83.4 0.6 copy-start.2
  84.8 3.5 %copy-start.4 = (bf16[32,2048]{1,0:T(8,128)(2,1)S(1)}, bf16[32,2048]{1,0:T(8,128)(2,1)}, u32[]{:S(2)}) copy-start(bf16[32,2048]{1,0:T(8,128)(2,1)} %fusion.13) | copy-start | bytes 393220
  84.8 163.5 %all-gather.3.cloned.1.call-start = ((), (), s32[]{:S(2)}) async-start(), calls=%async_computation.6 | async-start | bytes 9469952 | tf_op jit(solution)/shard_map/all_gather | solution.py:28
  87.4 0.8 copy-start.11
  90.4 59.7 %all-to-all-start.2 = ((bf16[32,12,2048]{2,1,0:T(8,128)(2,1)}), bf16[32,12,2048]{2,1,0:T(8,128)(2,1)S(1)}, u32[]{:S(2)}, u32[]{:S(2)}) async-start(bf16[32,12,2048]{2,1,0:T(8,128)(2,1)} %reshape.155), calls=%async_computation.2 | async-start | bytes 4194304 | tf_op jit(solution)/shard_map/all_to_all | solution.py:88
  153.0 105.9 %all-to-all-start.4 = ((bf16[16,512,176]{1,2,0:T(8,128)(2,1)}), bf16[16,512,176]{1,2,0:T(8,128)(2,1)}, u32[]{:S(2)}, u32[]{:S(2)}) async-start(bf16[16,512,176]{1,2,0:T(8,128)(2,1)} %stack.2), calls=%async_computation.4 | async-start | bytes 5767168 | tf_op jit(solution)/shard_map/all_to_all | solution.py:108
  258.9 58.5 %all-to-all-start.3 = ((bf16[32,12,2048]{2,1,0:T(8,128)(2,1)}), bf16[32,12,2048]{2,1,0:T(8,128)(2,1)S(1)}, u32[]{:S(2)}, u32[]{:S(2)}) async-start(bf16[32,12,2048]{2,1,0:T(8,128)(2,1)} %reshape.159), calls=%async_computation.3 | async-start | bytes 4194304 | tf_op jit(solution)/shard_map/all_to_all | solution.py:95
  317.3 6.6 %copy-start.1 = (bf16[32,12,2048]{2,1,0:T(8,128)(2,1)}, bf16[32,12,2048]{2,1,0:T(8,128)(2,1)S(1)}, u32[]{:S(2)}) copy-start(bf16[32,12,2048]{2,1,0:T(8,128)(2,1)S(1)} %all-to-all-done.3) | copy-start | bytes 4718596
  317.3 17.9 %all-to-all-start.5 = ((f32[16,32,128]{2,1,0:T(8,128)}), f32[16,32,128]{2,1,0:T(8,128)}, u32[]{:S(2)}, u32[]{:S(2)}) async-start(f32[16,32,128]{2,1,0:T(8,128)} %fusion.5), calls=%async_computation.5 | async-start | bytes 524288 | tf_op jit(solution)/shard_map/all_to_all | solution.py:113
  327.2 3.6 %copy-start.9 = (pred[32,6]{1,0:T(8,128)(4,1)S(1)}, pred[32,6]{1,0:T(8,128)(4,1)}, u32[]{:S(2)}) copy-start(pred[32,6]{1,0:T(8,128)(4,1)} %copy.37) | copy-start | bytes 580
  329.3 5.9 %copy-start.3 = (bf16[32,2048]{1,0:T(8,128)(2,1)S(1)}, bf16[32,2048]{1,0:T(8,128)(2,1)}, u32[]{:S(2)}) copy-start(bf16[32,2048]{1,0:T(8,128)(2,1)} %copy-done.2) | copy-start | bytes 393220
  329.3 7.0 %copy-start.12 = (f32[2048]{0:T(1024)S(1)}, f32[2048]{0:T(1024)}, u32[]{:S(2)}) copy-start(f32[2048]{0:T(1024)} %param.23) | copy-start | bytes 24580
Sparse Core Ops, SparseCore 0:
  84.9 39.6 all-gather.4
  126.8 121.4 all-gather.2
